TPU v7x, 32 devices: a whole 2x2x4 slice. The times are simulated.
32 devices in a mesh: tm: 8 (over z, y), cal: 4 (over x, core).
Axes of the slice: x: 2, y: 2, z: 4, core: 2. Of those that a mesh axis runs over, the one named last changes fastest.
Arguments:
- src_design: float32 [5, 4096, 128], P(None, ('tm', 'cal')), may hold values from -6 to 6
- att_design: float32 [3, 4096, 128], P(None, ('tm', 'cal')), may hold values from -6 to 6
- obs_phase: float32 [4096, 128], P(('tm', 'cal')), may hold values from 0 to 1
- cal_design: float32 [4096, 128], P(('tm', 'cal')), may hold values from -6 to 6
- obs_weight: float32 [4096, 128], P(('tm', 'cal')), may hold values from 0.1 to 12
- knot_index: int32 [4096, 128], P(('tm', 'cal')), may hold values from 0 to 4092, as said below
- cal_block: int32 [4096, 128], P(('tm', 'cal')), may hold values from 0 to 7
- cal_column: int32 [4096, 128], P(('tm', 'cal')), may hold values from 0 to 4095
- obs_count: int32 [4096], P(('tm', 'cal')), may hold values from 32 to 128
- src_res: float32 [5, 4096], P(None, ('tm', 'cal')), may hold values from -6 to 6
- att_res: float32 [3, 4096], P(None, ('tm', 'cal')), may hold values from -6 to 6
- cal_res: float32 [8, 4096], P('cal'), may hold values from -6 to 6
- src_dir: float32 [5, 4096], P(None, ('tm', 'cal')), may hold values from -6 to 6
- att_dir: float32 [3, 4096], P(None, ('tm', 'cal')), may hold values from -6 to 6
- cal_dir: float32 [8, 4096], P('cal'), may hold values from -6 to 6
Outputs:
- new_src_res: float32 [5, 4096], P(None, ('tm', 'cal'))
- new_att_res: float32 [3, 4096], P(None, ('tm', 'cal'))
- new_cal_res: float32 [8, 4096], P('cal')
- new_src_dir: float32 [5, 4096], P(None, ('tm', 'cal'))
- new_att_dir: float32 [3, 4096], P(None, ('tm', 'cal'))
- new_cal_dir: float32 [8, 4096], P('cal')
Inputs may be any that keep to these rules, and one draw needn't show every extreme that they name: The observations of source row s have knot intervals from (s // 128) * 128 to (s // 128) * 128 + 127, and knot_index + 3 < 4096.
All inputs are finite; a program needn't handle non-finite values.
Results may differ from a plain program's by a relative error of at most 0.00015.
Values sent between devices are 32-bit elements; how exact they have to be, the bound alone decides.
No kernel may reach another device: no remote copies, remote signals or barrier semaphores. Data moves between devices by JAX's collectives and lax.ppermute only.
A program may use at most 64 MiB of HBM per device.

v0:
```python
import jax
import jax.numpy as jnp
from jax import lax
from jax.sharding import PartitionSpec as P

EXACT = lax.Precision.HIGHEST


def passed_along(block, axis, distance):
    devices = range(lax.axis_size(axis))
    route = [(i - distance, i) for i in devices if i - distance in devices]
    return lax.ppermute(block, axis, route)


def spline(phase):
    rest = 1.0 - phase
    cube = phase * phase * phase
    square = phase * phase
    first = rest * rest * rest / 6.0
    second = (3.0 * cube - 6.0 * square + 4.0) / 6.0
    third = (-3.0 * cube + 3.0 * square + 3.0 * phase + 1.0) / 6.0
    fourth = cube / 6.0
    return (first, second, third, fourth)


def local(
    src_design,
    att_design,
    obs_phase,
    cal_design,
    obs_weight,
    knot_index,
    cal_block,
    cal_column,
    obs_count,
    src_res,
    att_res,
    cal_res,
    src_dir,
    att_dir,
    cal_dir,
):
    knot_count = att_dir.shape[1]
    blocks, col_width = cal_dir.shape
    all_blocks = blocks * lax.axis_size("cal")
    cal_size = all_blocks * col_width
    lane = 128
    rows = cal_size // lane
    src_rows, slots = obs_phase.shape
    first_row = (lax.axis_index("tm") == 0).astype(jnp.float32)
    cal_values = lax.all_gather(cal_dir, "cal", axis=0, tiled=True)
    edge_knots = passed_along(att_dir[:, :3], ("tm", "cal"), -1)
    att_ext = jnp.concatenate([att_dir, edge_knots], axis=1)
    live_mask = (lax.broadcasted_iota(jnp.int32, obs_phase.shape, 1) < obs_count[:, None]).astype(
        jnp.float32
    )
    basis = spline(obs_phase)
    local_knot = knot_index - lax.axis_index(("tm", "cal")) * knot_count
    knot_iota = lax.broadcasted_iota(jnp.int32, (knot_count, 1, 1), 0)
    knot_hot = (local_knot[None] == knot_iota).astype(jnp.float32)
    table = jnp.stack([att_ext[:, m : m + knot_count].T for m in range(4)], axis=1)
    table = table.reshape(knot_count, 12)
    picked = jnp.einsum("jq,jso->qso", table, knot_hot, precision=EXACT).reshape(
        4, 3, src_rows, slots
    )
    y_att = jnp.zeros_like(obs_phase)
    for m in range(4):
        y_att = y_att + basis[m] * jnp.sum(att_design * picked[m], axis=0)
    flat_index = cal_block * col_width + cal_column
    high = flat_index // lane
    low = flat_index % lane
    high_hot = (high[None] == lax.broadcasted_iota(jnp.int32, (rows, 1, 1), 0)).astype(jnp.float32)
    low_hot = (low[None] == lax.broadcasted_iota(jnp.int32, (lane, 1, 1), 0)).astype(jnp.float32)
    cal_table = cal_values.reshape(rows, lane)
    row_vals = jnp.einsum("hl,hso->lso", cal_table, high_hot, precision=EXACT)
    y_cal = cal_design * jnp.sum(row_vals * low_hot, axis=0)
    y_src = jnp.sum(src_design * src_dir[:, :, None], axis=0)
    response = live_mask * (y_src + y_att + y_cal)
    weighted = obs_weight * response
    curv_local = jnp.sum(weighted * response)
    norm_local = (
        jnp.sum(src_res * src_res)
        + jnp.sum(att_res * att_res)
        + first_row * jnp.sum(cal_res * cal_res)
    )
    q_src = jnp.sum(src_design * weighted[None], axis=2)
    scaled = att_design * weighted[None]
    spread = jnp.stack([basis[m][None] * scaled for m in range(4)], axis=0).reshape(
        12, src_rows, slots
    )
    gathered = jnp.einsum("qso,jso->jq", spread, knot_hot, precision=EXACT).reshape(
        knot_count, 4, 3
    )
    grad_ext = jnp.zeros((3, knot_count + 3), jnp.float32)
    for m in range(4):
        grad_ext = grad_ext + jnp.pad(gathered[:, m, :].T, ((0, 0), (m, 3 - m)))
    incoming = passed_along(grad_ext[:, knot_count:], ("tm", "cal"), 1)
    q_att = jnp.concatenate([grad_ext[:, :3] + incoming, grad_ext[:, 3:knot_count]], axis=1)
    cal_weighted = (cal_design * weighted)[None] * low_hot
    cal_term = jnp.einsum("hso,lso->hl", high_hot, cal_weighted, precision=EXACT)
    scalars = jnp.zeros((1, lane), jnp.float32).at[0, 0].set(norm_local).at[0, 1].set(curv_local)
    packed = jnp.concatenate([cal_term, scalars], axis=0)
    summed = lax.psum(packed, ("tm", "cal"))
    norm_now = summed[rows, 0]
    curvature = summed[rows, 1]
    own = lax.axis_index("cal") * (blocks * col_width // lane)
    q_cal = lax.dynamic_slice_in_dim(summed, own, blocks * col_width // lane, 0).reshape(
        blocks, col_width
    )
    step_len = norm_now / curvature
    new_src_res = src_res - step_len * q_src
    new_att_res = att_res - step_len * q_att
    new_cal_res = cal_res - step_len * q_cal
    next_local = (
        jnp.sum(new_src_res * new_src_res)
        + jnp.sum(new_att_res * new_att_res)
        + first_row * jnp.sum(new_cal_res * new_cal_res)
    )
    norm_next = lax.psum(jnp.zeros((1, lane), jnp.float32).at[0, 0].set(next_local), ("tm", "cal"))[
        0, 0
    ]
    ratio = norm_next / norm_now
    return (
        new_src_res,
        new_att_res,
        new_cal_res,
        new_src_res + ratio * src_dir,
        new_att_res + ratio * att_dir,
        new_cal_res + ratio * cal_dir,
    )


def solution(mesh):
    return jax.shard_map(
        local,
        mesh=mesh,
        in_specs=(
            P(None, ("tm", "cal"), None),
            P(None, ("tm", "cal"), None),
            P(("tm", "cal"), None),
            P(("tm", "cal"), None),
            P(("tm", "cal"), None),
            P(("tm", "cal"), None),
            P(("tm", "cal"), None),
            P(("tm", "cal"), None),
            P(("tm", "cal")),
            P(None, ("tm", "cal")),
            P(None, ("tm", "cal")),
            P("cal", None),
            P(None, ("tm", "cal")),
            P(None, ("tm", "cal")),
            P("cal", None),
        ),
        out_specs=(
            P(None, ("tm", "cal")),
            P(None, ("tm", "cal")),
            P("cal", None),
            P(None, ("tm", "cal")),
            P(None, ("tm", "cal")),
            P("cal", None),
        ),
        check_vma=False,
    )
```

profile of v0, /device:TPU:0, one launch (start us, length us, event | category | flops | bytes accessed | tf_op | source)
XLA Modules:
  0.0 323.5 jit_solution(16515309153429786869)
XLA Ops:
  7.2 1.3 collective-permute-start
  10.5 1.4 multiply_reduce_fusion.4
  11.9 1.3 multiply_reduce_fusion.8
  13.2 1.3 multiply_reduce_fusion.6
  17.7 0.8 broadcast_subtract_fusion
  18.6 7.7 %all-gather = f32[4,2,4096]{2,1,0:T(2,128)S(1)} all-gather(f32[1,2,4096]{2,1,0:T(2,128)} %bitcast.78), channel_id=1, replica_groups=mesh['tm'=8,'cal'=4] {'cal'}, dimensions={0}, use_global_device_ids=true | all-gather | bytes 163840 | tf_op jit(solution)/shard_map/all_gather | solution.py:51
  26.4 0.9 add_select_fusion.1
  27.4 1.3 iota_compare_fusion.1
  28.7 38.5 %copy.50 = pred[128,128,128]{2,0,1:T(32,128)(4,1)S(1)} copy(pred[128,128,128]{1,0,2:T(32,128)(4,1)S(1)} %iota_compare_fusion.1) | data formatting | bytes 4194304 | tf_op jit(solution)/shard_map/eq | solution.py:60
  67.2 2.7 iota_compare_fusion
  70.0 20.5 %copy.55 = pred[256,128,128]{2,0,1:T(32,128)(4,1)} copy(pred[256,128,128]{1,0,2:T(32,128)(4,1)S(1)} %iota_compare_fusion) | data formatting | bytes 8388608 | tf_op jit(solution)/shard_map/eq | solution.py:72
  90.7 8.2 %fusion = f32[128,128]{1,0:T(8,128)S(1)} fusion(s32[128,128]{1,0:T(8,128)S(1)} %get-tuple-element.62, pred[256,128,128]{2,0,1:T(32,128)(4,1)} %copy.55, f32[256,128]{1,0:T(8,128)S(1)} %reshape.140), kind=kOutput, calls=%fused_computation.2 | convolution fusion | flops 6448726016 | bytes 4456448 | tf_op jit(solution)/shard_map/hl,hso->lso/dot_general | solution.py:75
  99.1 2.2 fusion.29
  101.3 0.8 fusion.7
  102.9 4.2 %fusion.4 = f32[128,4,3]{0,1,2:T(4,128)S(1)} fusion(f32[4,3,128,128]{3,0,2,1:T(4,128)S(1)} %copy.59, s32[128,128]{0,1:T(8,128)S(1)} %copy.49), kind=kOutput, calls=%fused_computation.9 | convolution fusion | flops 304087040 | bytes 858112 | tf_op jit(solution)/shard_map/qso,jso->jq/dot_general | solution.py:91
  107.9 2.2 collective-permute-start.1
  110.1 4.7 %fusion.1 = f32[128,128,128]{2,0,1:T(8,128)} fusion(f32[128,128]{1,0:T(8,128)S(1)} %get-tuple-element.52, s32[128,128]{1,0:T(8,128)S(1)} %get-tuple-element.62), kind=kLoop, calls=%fused_computation.5 | loop fusion | flops 4194304 | bytes 8519680 | tf_op jit(solution)/shard_map/mul | solution.py:99
  114.8 9.3 %copy.57 = f32[128,128,128]{1,0,2:T(8,128)} copy(f32[128,128,128]{2,0,1:T(8,128)} %fusion.1) | data formatting | bytes 16777216 | tf_op jit(solution)/shard_map/mul | solution.py:99
  124.2 11.2 %convolution_bitcast_fusion = f32[256,128]{1,0:T(8,128)S(1)} fusion(f32[128,128,128]{1,0,2:T(8,128)} %copy.57, s32[128,128]{0,1:T(8,128)S(1)} %copy.48), kind=kOutput, calls=%fused_computation.8 | convolution fusion | flops 6446645248 | bytes 8585216 | tf_op jit(solution)/shard_map/hso,lso->hl/dot_general | solution.py:100
  135.3 2.5 fusion.28
  137.9 1.4 scatter.11
  140.0 123.3 %all-reduce.8.cloned.1.call-done = f32[257,128]{1,0:T(8,128)} async-done(((f32[257,128]{1,0:T(8,128)}), f32[257,128]{1,0:T(8,128)}) %all-reduce.8.cloned.1.call-update) | async-done | bytes 131600 | tf_op jit(solution)/shard_map/psum | solution.py:103
  263.3 1.3 fusion.26
  271.6 42.5 %psum.15 = f32[1,128]{1,0:T(1,128)S(1)} all-reduce(f32[1,128]{1,0:T(1,128)S(1)} %scatter.14), channel_id=1, replica_groups=mesh['tm'=8,'cal'=4] {'tm','cal'}, use_global_device_ids=true, to_apply=%region_17.18 | all-reduce | flops 128 | bytes 1024 | tf_op jit(solution)/shard_map/psum | solution.py:119
  (71 shorter events, 10.1 us)
Async XLA Ops:
  7.2 256.2 %all-reduce.8.cloned.1.call-start = ((), (), s32[]{:S(2)}) async-start(), calls=%async_computation | async-start | bytes 270336 | tf_op jit(solution)/shard_map/psum | solution.py:103
  7.2 91.8 %collective-permute-start = (f32[3,3]{1,0:T(4,128)}, f32[3,3]{1,0:T(4,128)S(1)}, u32[]{:S(2)}, u32[]{:S(2)}) collective-permute-start(f32[3,3]{1,0:T(4,128)} %bitcast.79), channel_id=1, source_target_pairs={{1,0},{2,1},{3,2},{4,3},{5,4},{6,5},{7,6},{8,7},{9,8},{10,9},{11,1... | collective-permute-start | bytes 116 | tf_op jit(solution)/shard_map/ppermute | solution.py:12
  69.9 20.6 %copy-start = (f32[5,128,128]{2,1,0:T(8,128)S(1)}, f32[5,128,128]{2,1,0:T(8,128)}, u32[]{:S(2)}) copy-start(f32[5,128,128]{2,1,0:T(8,128)} %param.21) | copy-start | bytes 983044
  69.9 20.6 %copy-start.9 = (f32[5,128]{1,0:T(8,128)S(1)}, f32[5,128]{1,0:T(8,128)}, u32[]{:S(2)}) copy-start(f32[5,128]{1,0:T(8,128)} %param.33) | copy-start | bytes 7684
  90.7 8.4 %copy-start.8 = (f32[3,128]{1,0:T(4,128)S(1)}, f32[3,128]{1,0:T(4,128)}, u32[]{:S(2)}) copy-start(f32[3,128]{1,0:T(4,128)} %param.34) | copy-start | bytes 4612
  90.7 10.6 %copy-start.1 = (f32[3,128,128]{2,1,0:T(8,128)S(1)}, f32[3,128,128]{2,1,0:T(8,128)}, u32[]{:S(2)}) copy-start(f32[3,128,128]{2,1,0:T(8,128)} %param.22) | copy-start | bytes 589828
  98.9 3.2 copy-start.5
  98.9 3.2 copy-start.6
  98.9 3.2 copy-start.7
  99.0 3.2 copy-start.14
  107.9 32.1 %collective-permute-start.1 = (f32[3,3]{1,0:T(4,128)S(1)}, f32[3,3]{1,0:T(4,128)S(1)}, u32[]{:S(2)}, u32[]{:S(2)}) collective-permute-start(f32[3,3]{1,0:T(4,128)S(1)} %slice.142), channel_id=1, source_target_pairs={{0,1},{1,2},{2,3},{3,4},{4,5},{5,6},{6,7},{7,8},{8,9},{9,10},{10,1... | collective-permute-start | bytes 116 | tf_op jit(solution)/shard_map/ppermute | solution.py:12
  124.2 142.6 %copy-start.11 = (f32[5,128]{1,0:T(8,128)S(1)}, f32[5,128]{1,0:T(8,128)}, u32[]{:S(2)}) copy-start(f32[5,128]{1,0:T(8,128)} %param.30) | copy-start | bytes 7684
  124.2 143.3 %copy-start.4 = (f32[2,4096]{1,0:T(2,128)S(1)}, f32[2,4096]{1,0:T(2,128)}, u32[]{:S(2)}) copy-start(f32[2,4096]{1,0:T(2,128)} %param.32) | copy-start | bytes 98308
  124.2 144.7 %copy-start.12 = (f32[3,128]{1,0:T(4,128)S(1)}, f32[3,128]{1,0:T(4,128)}, u32[]{:S(2)}) copy-start(f32[3,128]{1,0:T(4,128)} %param.31) | copy-start | bytes 4612
  124.2 191.8 %copy-start.2 = (f32[2,4096]{1,0:T(2,128)S(1)}, f32[2,4096]{1,0:T(2,128)}, u32[]{:S(2)}) copy-start(f32[2,4096]{1,0:T(2,128)} %param.35) | copy-start | bytes 98308
  267.4 49.2 %copy-start.10 = (f32[5,128]{1,0:T(8,128)}, f32[5,128]{1,0:T(8,128)S(1)}, u32[]{:S(2)}) copy-start(f32[5,128]{1,0:T(8,128)S(1)} %get-tuple-element.51) | copy-start | bytes 7684
  268.1 48.5 %copy-start.3 = (f32[2,4096]{1,0:T(2,128)}, f32[2,4096]{1,0:T(2,128)S(1)}, u32[]{:S(2)}) copy-start(f32[2,4096]{1,0:T(2,128)S(1)} %get-tuple-element.47) | copy-start | bytes 98308
  269.6 47.1 %copy-start.13 = (f32[3,128]{1,0:T(4,128)}, f32[3,128]{1,0:T(4,128)S(1)}, u32[]{:S(2)}) copy-start(f32[3,128]{1,0:T(4,128)S(1)} %get-tuple-element.49) | copy-start | bytes 4612
Sparse Core Ops, SparseCore 0:
  140.1 123.1 all-reduce.7
where the time goes:
time: 324 us
  waiting for transfers between devices  123 us (38%)
  local copies, waits for them, and re-layouts  73.3 us (23%)
  blocking collectives  50.1 us (15%)
  matrix products  25.8 us (8%)
  other arithmetic  25.7 us (8%)
  between operations  21.7 us (7%)
  starting transfers between devices  3.56 us (1%)
    psum x1, waiting for transfers between devices, local(): summed = lax.psum(packed, ('tm', 'cal'))  123 us
    psum x1, blocking collectives, local(): lax.psum(jnp.zeros((1, lane), jnp.float32).at[0, 0].set(next_local), ('tm...  42.5 us
    eq x1, local copies, waits for them, and re-layouts, local(): knot_hot = (local_knot[None] == knot_iota).astype(jnp.float32)  38.5 us
    eq x1, local copies, waits for them, and re-layouts, local(): high[None] == lax.broadcasted_iota(jnp.int32, (rows, 1, 1), 0)  20.5 us
    dot_general x1, matrix products, local(): jnp.einsum('hso,lso->hl', high_hot, cal_weighted, precision=EXACT)  11.2 us
    mul x1, local copies, waits for them, and re-layouts, local(): cal_weighted = (cal_design * weighted)[None] * low_hot  9.32 us
    dot_general x1, matrix products, local(): row_vals = jnp.einsum('hl,hso->lso', cal_table, high_hot, precision=EXACT)  8.23 us
    all_gather x1, blocking collectives, local(): cal_values = lax.all_gather(cal_dir, 'cal', axis=0, tiled=True)  7.65 us
  transfers between devices with their start and end apart: 3, of which 1 were waited for; matrix products, arithmetic and copies ran while one was open for 34% of the time, Pallas kernels for 0%

commit v1 on v0

--- a/solution.py
+++ b/solution.py
@@ -116,9 +116,10 @@
         + jnp.sum(new_att_res * new_att_res)
         + first_row * jnp.sum(new_cal_res * new_cal_res)
     )
-    norm_next = lax.psum(jnp.zeros((1, lane), jnp.float32).at[0, 0].set(next_local), ("tm", "cal"))[
-        0, 0
-    ]
+    norm_next = jnp.sum(
+        lax.all_gather(jnp.zeros((1, lane), jnp.float32).at[0, 0].set(next_local), ("tm", "cal")),
+        axis=0,
+    )[0, 0]
     ratio = norm_next / norm_now
     return (
         new_src_res,

time: 324 us -> 324 us (level)
    all_gather x0 -> x1, blocking collectives: none -> 42.5 us  [local(): lax.all_gather(jnp.zeros((1, lane), jnp.float32).at[0, 0].set(next_local)...]
    psum x1 -> x0, blocking collectives: 42.5 us -> none  [local(): lax.psum(jnp.zeros((1, lane), jnp.float32).at[0, 0].set(next_local), ('tm...]
where the time goes in v1:
time: 324 us
  waiting for transfers between devices  123 us (38%)
  local copies, waits for them, and re-layouts  73.3 us (23%)
  blocking collectives  50.2 us (15%)
  other arithmetic  25.8 us (8%)
  matrix products  25.7 us (8%)
  between operations  21.7 us (7%)
  starting transfers between devices  3.56 us (1%)
    psum x1, waiting for transfers between devices, local(): summed = lax.psum(packed, ('tm', 'cal'))  123 us
    all_gather x1, blocking collectives, local(): lax.all_gather(jnp.zeros((1, lane), jnp.float32).at[0, 0].set(next_local)...  42.5 us
    eq x1, local copies, waits for them, and re-layouts, local(): knot_hot = (local_knot[None] == knot_iota).astype(jnp.float32)  38.6 us
    eq x1, local copies, waits for them, and re-layouts, local(): high[None] == lax.broadcasted_iota(jnp.int32, (rows, 1, 1), 0)  20.5 us
    dot_general x1, matrix products, local(): jnp.einsum('hso,lso->hl', high_hot, cal_weighted, precision=EXACT)  11.2 us
    mul x1, local copies, waits for them, and re-layouts, local(): cal_weighted = (cal_design * weighted)[None] * low_hot  9.32 us
    dot_general x1, matrix products, local(): row_vals = jnp.einsum('hl,hso->lso', cal_table, high_hot, precision=EXACT)  8.24 us
    all_gather x1, blocking collectives, local(): cal_values = lax.all_gather(cal_dir, 'cal', axis=0, tiled=True)  7.65 us
  transfers between devices with their start and end apart: 3, of which 1 were waited for; matrix products, arithmetic and copies ran while one was open for 34% of the time, Pallas kernels for 0%

profile of v1, /device:TPU:0, one launch (start us, length us, event | category | flops | bytes accessed | tf_op | source)
XLA Modules:
  0.0 323.6 jit_solution(1761260230932469994)
XLA Ops:
  7.2 1.3 collective-permute-start
  10.5 1.4 multiply_reduce_fusion.4
  11.9 1.3 multiply_reduce_fusion.8
  13.2 1.3 multiply_reduce_fusion.6
  17.7 0.8 broadcast_subtract_fusion
  18.6 7.7 %all-gather.1 = f32[4,2,4096]{2,1,0:T(2,128)S(1)} all-gather(f32[1,2,4096]{2,1,0:T(2,128)} %bitcast.81), channel_id=1, replica_groups=mesh['tm'=8,'cal'=4] {'cal'}, dimensions={0}, use_global_device_ids=true | all-gather | bytes 163840 | tf_op jit(solution)/shard_map/all_gather | solution.py:51
  26.4 0.9 add_select_fusion.1
  27.4 1.3 iota_compare_fusion.1
  28.7 38.6 %copy.50 = pred[128,128,128]{2,0,1:T(32,128)(4,1)S(1)} copy(pred[128,128,128]{1,0,2:T(32,128)(4,1)S(1)} %iota_compare_fusion.1) | data formatting | bytes 4194304 | tf_op jit(solution)/shard_map/eq | solution.py:60
  67.3 2.7 iota_compare_fusion
  70.0 20.5 %copy.55 = pred[256,128,128]{2,0,1:T(32,128)(4,1)} copy(pred[256,128,128]{1,0,2:T(32,128)(4,1)S(1)} %iota_compare_fusion) | data formatting | bytes 8388608 | tf_op jit(solution)/shard_map/eq | solution.py:72
  90.8 8.2 %fusion = f32[128,128]{1,0:T(8,128)S(1)} fusion(s32[128,128]{1,0:T(8,128)S(1)} %get-tuple-element.62, pred[256,128,128]{2,0,1:T(32,128)(4,1)} %copy.55, f32[256,128]{1,0:T(8,128)S(1)} %reshape.141), kind=kOutput, calls=%fused_computation.2 | convolution fusion | flops 6448726016 | bytes 4456448 | tf_op jit(solution)/shard_map/hl,hso->lso/dot_general | solution.py:75
  99.2 2.1 fusion.29
  101.3 0.8 fusion.7
  102.9 4.2 %fusion.4 = f32[128,4,3]{0,1,2:T(4,128)S(1)} fusion(f32[4,3,128,128]{3,0,2,1:T(4,128)S(1)} %copy.59, s32[128,128]{0,1:T(8,128)S(1)} %copy.49), kind=kOutput, calls=%fused_computation.9 | convolution fusion | flops 304087040 | bytes 858112 | tf_op jit(solution)/shard_map/qso,jso->jq/dot_general | solution.py:91
  107.9 2.2 collective-permute-start.1
  110.2 4.7 %fusion.1 = f32[128,128,128]{2,0,1:T(8,128)} fusion(f32[128,128]{1,0:T(8,128)S(1)} %get-tuple-element.52, s32[128,128]{1,0:T(8,128)S(1)} %get-tuple-element.62), kind=kLoop, calls=%fused_computation.5 | loop fusion | flops 4194304 | bytes 8519680 | tf_op jit(solution)/shard_map/mul | solution.py:99
  114.9 9.3 %copy.57 = f32[128,128,128]{1,0,2:T(8,128)} copy(f32[128,128,128]{2,0,1:T(8,128)} %fusion.1) | data formatting | bytes 16777216 | tf_op jit(solution)/shard_map/mul | solution.py:99
  124.2 11.2 %convolution_bitcast_fusion = f32[256,128]{1,0:T(8,128)S(1)} fusion(f32[128,128,128]{1,0,2:T(8,128)} %copy.57, s32[128,128]{0,1:T(8,128)S(1)} %copy.48), kind=kOutput, calls=%fused_computation.8 | convolution fusion | flops 6446645248 | bytes 8585216 | tf_op jit(solution)/shard_map/hso,lso->hl/dot_general | solution.py:100
  135.4 2.5 fusion.28
  137.9 1.4 scatter.11
  140.0 123.3 %all-reduce.8.cloned.1.call-done = f32[257,128]{1,0:T(8,128)} async-done(((f32[257,128]{1,0:T(8,128)}), f32[257,128]{1,0:T(8,128)}) %all-reduce.8.cloned.1.call-update) | async-done | bytes 131600 | tf_op jit(solution)/shard_map/psum | solution.py:103
  263.3 1.3 fusion.26
  271.6 42.5 %all-gather.2 = f32[32,1,128]{2,1,0:T(1,128)S(1)} all-gather(f32[1,1,128]{2,1,0:T(1,128)S(1)} %pad_bitcast_fusion), channel_id=2, replica_groups=mesh['tm'=8,'cal'=4] {'tm','cal'}, dimensions={0}, use_global_device_ids=true | all-gather | bytes 16896 | tf_op jit(solution)/shard_map/all_gather | solution.py:120
  (72 shorter events, 10.1 us)
Async XLA Ops:
  7.2 256.2 %all-reduce.8.cloned.1.call-start = ((), (), s32[]{:S(2)}) async-start(), calls=%async_computation | async-start | bytes 270336 | tf_op jit(solution)/shard_map/psum | solution.py:103
  7.2 91.8 %collective-permute-start = (f32[3,3]{1,0:T(4,128)}, f32[3,3]{1,0:T(4,128)S(1)}, u32[]{:S(2)}, u32[]{:S(2)}) collective-permute-start(f32[3,3]{1,0:T(4,128)} %bitcast.82), channel_id=1, source_target_pairs={{1,0},{2,1},{3,2},{4,3},{5,4},{6,5},{7,6},{8,7},{9,8},{10,9},{11,1... | collective-permute-start | bytes 116 | tf_op jit(solution)/shard_map/ppermute | solution.py:12
  70.0 20.6 %copy-start = (f32[5,128,128]{2,1,0:T(8,128)S(1)}, f32[5,128,128]{2,1,0:T(8,128)}, u32[]{:S(2)}) copy-start(f32[5,128,128]{2,1,0:T(8,128)} %param.21) | copy-start | bytes 983044
  70.0 20.6 %copy-start.9 = (f32[5,128]{1,0:T(8,128)S(1)}, f32[5,128]{1,0:T(8,128)}, u32[]{:S(2)}) copy-start(f32[5,128]{1,0:T(8,128)} %param.33) | copy-start | bytes 7684
  90.7 8.4 %copy-start.8 = (f32[3,128]{1,0:T(4,128)S(1)}, f32[3,128]{1,0:T(4,128)}, u32[]{:S(2)}) copy-start(f32[3,128]{1,0:T(4,128)} %param.34) | copy-start | bytes 4612
  90.7 10.6 %copy-start.1 = (f32[3,128,128]{2,1,0:T(8,128)S(1)}, f32[3,128,128]{2,1,0:T(8,128)}, u32[]{:S(2)}) copy-start(f32[3,128,128]{2,1,0:T(8,128)} %param.22) | copy-start | bytes 589828
  99.0 3.2 copy-start.5
  99.0 3.2 copy-start.6
  99.0 3.2 copy-start.7
  99.0 3.2 copy-start.14
  107.9 32.1 %collective-permute-start.1 = (f32[3,3]{1,0:T(4,128)S(1)}, f32[3,3]{1,0:T(4,128)S(1)}, u32[]{:S(2)}, u32[]{:S(2)}) collective-permute-start(f32[3,3]{1,0:T(4,128)S(1)} %slice.142), channel_id=1, source_target_pairs={{0,1},{1,2},{2,3},{3,4},{4,5},{5,6},{6,7},{7,8},{8,9},{9,10},{10,1... | collective-permute-start | bytes 116 | tf_op jit(solution)/shard_map/ppermute | solution.py:12
  124.2 142.6 %copy-start.11 = (f32[5,128]{1,0:T(8,128)S(1)}, f32[5,128]{1,0:T(8,128)}, u32[]{:S(2)}) copy-start(f32[5,128]{1,0:T(8,128)} %param.30) | copy-start | bytes 7684
  124.2 143.2 %copy-start.4 = (f32[2,4096]{1,0:T(2,128)S(1)}, f32[2,4096]{1,0:T(2,128)}, u32[]{:S(2)}) copy-start(f32[2,4096]{1,0:T(2,128)} %param.32) | copy-start | bytes 98308
  124.2 144.6 %copy-start.12 = (f32[3,128]{1,0:T(4,128)S(1)}, f32[3,128]{1,0:T(4,128)}, u32[]{:S(2)}) copy-start(f32[3,128]{1,0:T(4,128)} %param.31) | copy-start | bytes 4612
  124.2 191.9 %copy-start.2 = (f32[2,4096]{1,0:T(2,128)S(1)}, f32[2,4096]{1,0:T(2,128)}, u32[]{:S(2)}) copy-start(f32[2,4096]{1,0:T(2,128)} %param.35) | copy-start | bytes 98308
  267.4 49.3 %copy-start.10 = (f32[5,128]{1,0:T(8,128)}, f32[5,128]{1,0:T(8,128)S(1)}, u32[]{:S(2)}) copy-start(f32[5,128]{1,0:T(8,128)S(1)} %get-tuple-element.51) | copy-start | bytes 7684
  268.2 48.6 %copy-start.3 = (f32[2,4096]{1,0:T(2,128)}, f32[2,4096]{1,0:T(2,128)S(1)}, u32[]{:S(2)}) copy-start(f32[2,4096]{1,0:T(2,128)S(1)} %get-tuple-element.47) | copy-start | bytes 98308
  269.6 47.1 %copy-start.13 = (f32[3,128]{1,0:T(4,128)}, f32[3,128]{1,0:T(4,128)S(1)}, u32[]{:S(2)}) copy-start(f32[3,128]{1,0:T(4,128)S(1)} %get-tuple-element.49) | copy-start | bytes 4612
Sparse Core Ops, SparseCore 0:
  140.1 123.1 all-reduce.7
